TPU v7x, 256 devices: a whole 4x4x8 slice. The times are simulated.
256 devices in a mesh: seq: 64 (over z, y, core), mp: 4 (over x).
Axes of the slice: x: 4, y: 4, z: 8, core: 2. Of those that a mesh axis runs over, the one named last changes fastest.
Arguments:
- patches: bfloat16 [262144, 1280], P('seq'), may hold values from -2 to 2
- w_qkv: bfloat16 [1280, 3840], P('seq', 'mp'), as said below
- w_out: bfloat16 [1280, 1280], P('mp', 'seq'), may hold values from -0.15625 to 0.15625
- page_rows: int32 [64], replicated, may hold values from 32 to 64, as said below
- page_cols: int32 [64], replicated, may hold values from 32 to 64, as said below
- window_slot: int32 [64, 64], replicated, may hold values from 0 to 63, each once within a row
Outputs:
- blocks: bfloat16 [262144, 1280], P('seq', 'mp')
Inputs may be any that keep to these rules, and one draw needn't show every extreme that they name: `page_rows`: page heights, multiples of 16; some page has the largest. `page_cols`: page widths, multiples of 16; some page has the largest. `window_slot`: each row is a permutation. `w_qkv`: entries of order at most 5.5 / sqrt(1280).
All inputs are finite; a program needn't handle non-finite values.
Results may differ from a plain program's by a relative error of at most 0.012.
Values may be sent and summed in bfloat16 or wider, within the bound.
No kernel may reach another device: no remote copies, remote signals or barrier semaphores. Data moves between devices by JAX's collectives and lax.ppermute only.
A program may use at most 192 MiB of HBM per device.

v0:
```python
import jax
import jax.numpy as jnp
from jax import lax
from jax.sharding import PartitionSpec as P

HD = 80
WS = 8
QUARTERS = 4
EPSILON = 1e-06


def angle_tables(row_place, column_place, head_size):
    quarter = head_size // 4
    frequency = 1.0 / 10000.0 ** (jnp.arange(quarter, dtype=jnp.float32) * 2.0 / (head_size // 2))
    angles = jnp.concatenate(
        [
            row_place[..., None].astype(jnp.float32) * frequency,
            column_place[..., None].astype(jnp.float32) * frequency,
        ],
        axis=-1,
    )
    angles = jnp.concatenate([angles, angles], axis=-1)
    return (jnp.cos(angles), jnp.sin(angles))


def slot_positions(page_widths, slot_table, slot_numbers, window_side):
    matches = slot_table[:, :, None] == slot_numbers[None, None, :]
    ordinal = jnp.arange(slot_table.shape[1], dtype=jnp.int32)
    window = jnp.sum(jnp.where(matches, ordinal[None, :, None], 0), axis=1)
    across = page_widths // window_side
    window_row = window // across[:, None]
    window_column = window % across[:, None]
    unit_side = window_side // 2
    position = jnp.arange(window_side * window_side, dtype=jnp.int32)
    merge_unit = position // 4
    corner = position % 4
    inner_row = merge_unit // unit_side * 2 + corner // 2
    inner_column = merge_unit % unit_side * 2 + corner % 2
    row_place = window_row[:, :, None] * window_side + inner_row
    column_place = window_column[:, :, None] * window_side + inner_column
    return (row_place, column_place)


def block_sources(height, page_width, slot_row, block_count):
    across = page_width // WS
    block = jnp.arange(block_count, dtype=jnp.int32)
    band = block // across
    column = block % across
    window_row = band // QUARTERS
    quarter = band % QUARTERS
    live = window_row < height // WS
    window = jnp.where(live, window_row * across + column, 0)
    ordinal = jnp.arange(slot_row.shape[0], dtype=jnp.int32)
    slot = jnp.sum(jnp.where(window[:, None] == ordinal[None, :], slot_row[None, :], 0), axis=1)
    return (slot * QUARTERS + quarter, live)


def normalize(block_in):
    values = block_in.astype(jnp.float32)
    factor = lax.rsqrt(jnp.mean(values * values, axis=-1, keepdims=True) + EPSILON)
    return (values * factor).astype(jnp.bfloat16)


def rotated_columns(weight):
    half = weight.shape[-1] // 2
    return jnp.concatenate([-weight[..., half:], weight[..., :half]], axis=-1)


def local(patches, w_qkv, w_out, page_rows, page_cols, window_slot):
    seq_index = lax.axis_index("seq")
    seq_count = lax.axis_size("seq")
    mp_index = lax.axis_index("mp")
    page_count = window_slot.shape[0]
    slot_count = window_slot.shape[1]
    slots_held = slot_count // seq_count
    window_tokens = WS * WS
    quarter_tokens = window_tokens // QUARTERS
    model_width = patches.shape[1]
    windows = patches.shape[0] // window_tokens
    own_rows = w_qkv.shape[0]
    heads = w_qkv.shape[1] // (3 * HD)
    qkv = w_qkv.reshape(own_rows, heads, 3, HD)
    w_q = qkv[:, :, 0]
    w_k = qkv[:, :, 1]
    fused_rows = jnp.concatenate(
        [
            w_q.reshape(own_rows, heads * HD),
            w_k.reshape(own_rows, heads * HD),
            rotated_columns(w_q).reshape(own_rows, heads * HD),
            rotated_columns(w_k).reshape(own_rows, heads * HD),
            qkv[:, :, 2].reshape(own_rows, heads * HD),
            w_out.T,
        ],
        axis=1,
    )
    joined = lax.all_gather(fused_rows, "seq", axis=0, tiled=True)
    fused = joined[:, : 5 * heads * HD]
    out_rows_t = joined[:, 5 * heads * HD :]
    out_full_t = lax.all_gather(out_rows_t, "mp", axis=1, tiled=True)
    slot_numbers = seq_index * slots_held + jnp.arange(slots_held, dtype=jnp.int32)
    row_place, column_place = slot_positions(page_cols, window_slot, slot_numbers, WS)
    cosine, sine = angle_tables(
        row_place.reshape(-1, window_tokens), column_place.reshape(-1, window_tokens), HD
    )
    cosine = jnp.tile(cosine.reshape(-1, HD), (1, 2 * heads))
    sine = jnp.tile(sine.reshape(-1, HD), (1, 2 * heads))
    normed = normalize(patches)
    projected = jnp.dot(normed, fused, preferred_element_type=jnp.float32)
    width = heads * HD
    turned = projected[:, : 2 * width] * cosine + projected[:, 2 * width : 4 * width] * sine
    turned = turned.astype(jnp.bfloat16).reshape(windows, window_tokens, 2 * width)
    queries = turned[:, :, :width]
    key_block = turned[:, :, width:]
    values = projected[:, 4 * width :].astype(jnp.bfloat16).reshape(windows, window_tokens, width)
    lane_head = jnp.arange(width, dtype=jnp.int32) // HD
    scale = 1.0 / HD**0.5
    mixed = jnp.zeros((windows, window_tokens, width), jnp.float32)
    for head in range(heads):
        mask = lane_head == head
        picked = jnp.where(mask, queries, jnp.zeros_like(queries))
        scores = (
            jnp.einsum("wqd,wkd->wqk", picked, key_block, preferred_element_type=jnp.float32)
            * scale
        )
        row_max = jnp.max(scores, axis=-1, keepdims=True)
        lifted = jnp.exp(scores - row_max)
        weights = (lifted / jnp.sum(lifted, axis=-1, keepdims=True)).astype(jnp.bfloat16)
        own_values = jnp.where(mask, values, jnp.zeros_like(values))
        mixed = mixed + jnp.einsum(
            "wqk,wkd->wqd", weights, own_values, preferred_element_type=jnp.float32
        )
    mixed = mixed.astype(jnp.bfloat16)
    spread = mixed.reshape(windows, QUARTERS, quarter_tokens, width)
    gathered = lax.all_to_all(spread, "mp", split_axis=1, concat_axis=1, tiled=True)
    out_grouped = out_full_t.reshape(model_width, QUARTERS, width)
    branch = lax.dot_general(
        gathered, out_grouped, (((1, 3), (1, 2)), ((), ())), preferred_element_type=jnp.float32
    )
    branch = branch.reshape(windows * quarter_tokens, model_width)
    residual = patches.reshape(windows, QUARTERS, quarter_tokens, model_width)
    residual = lax.dynamic_index_in_dim(residual, mp_index, 1, keepdims=False)
    residual = residual.reshape(windows * quarter_tokens, model_width).astype(jnp.float32)
    block_out = (residual + branch).astype(jnp.bfloat16)
    share_width = model_width // QUARTERS
    sectioned = block_out.reshape(page_count, quarter_tokens, QUARTERS, share_width)
    sectioned = jnp.transpose(sectioned, (0, 2, 1, 3)).reshape(
        page_count * QUARTERS, quarter_tokens, share_width
    )
    landed = lax.all_to_all(sectioned, ("seq", "mp"), split_axis=0, concat_axis=0, tiled=True)
    own_pages = page_count // seq_count
    first_page = seq_index * own_pages
    heights = lax.dynamic_slice_in_dim(page_rows, first_page, own_pages, 0)
    widths = lax.dynamic_slice_in_dim(page_cols, first_page, own_pages, 0)
    slot_rows = lax.dynamic_slice_in_dim(window_slot, first_page, own_pages, 0)
    block_count = slot_count * QUARTERS // own_pages
    landed = landed.reshape(own_pages, block_count, quarter_tokens, share_width)

    def regroup(received, height, page_width, slot_row):
        source, live = block_sources(height, page_width, slot_row, block_count)
        picked = jnp.take(received, source, axis=0)
        return jnp.where(live[:, None, None], picked, jnp.zeros_like(picked))

    merged = jax.vmap(regroup)(landed, heights, widths, slot_rows)
    return merged.reshape(-1, share_width)


def solution(mesh):
    return jax.shard_map(
        local,
        mesh=mesh,
        in_specs=(P("seq", None), P("seq", "mp"), P("mp", "seq"), P(), P(), P()),
        out_specs=P("seq", "mp"),
        check_vma=False,
    )
```

profile of v0, /device:TPU:1, one launch (start us, length us, event | category | flops | bytes accessed | tf_op | source)
XLA Modules:
  0.0 355.9 jit_solution(10992189034661572990)
XLA Ops:
  12.5 6.1 %fusion.4 = f32[4096]{0:T(1024)S(1)} fusion(bf16[4096,1280]{1,0:T(8,128)(2,1)} %param.6), kind=kLoop, calls=%fused_computation.7 | loop fusion | flops 15724544 | bytes 10502144 | tf_op jit(solution)/shard_map/reduce_sum | solution.py:60
  18.7 4.8 %fusion.69 = (f32[4096,80]{0,1:T(8,128)S(1)}, f32[4096,80]{0,1:T(8,128)S(1)}) fusion(f32[4096,20]{0,1:T(8,128)S(1)} %get-tuple-element.19, f32[4096,20]{0,1:T(8,128)S(1)} %get-tuple-element.18), kind=kLoop, calls=%fused_computation.88 | loop fusion | flops 983040 | bytes 3276800 | tf_op jit(solution)/shard_map/cos | solution.py:23
  23.5 71.3 %all-gather.6.cloned.1.call-done = bf16[64,20,1920]{2,1,0:T(8,128)(2,1)} async-done(((bf16[1,20,1920]{2,1,0:T(8,128)(2,1)}), bf16[64,20,1920]{2,1,0:T(8,128)(2,1)}) %all-gather.6.cloned.1.call-update) | async-done | bytes 4915216 | tf_op jit(solution)/shard_map/all_gather | solution.py:96
  94.8 7.5 %reshape.662 = bf16[1280,1920]{1,0:T(8,128)(2,1)} reshape(bf16[64,20,1920]{2,1,0:T(8,128)(2,1)} %all-gather.6.cloned.1.call-done) | data formatting | bytes 9830400
  107.2 23.8 %fusion.6 = f32[4096,1600]{0,1:T(8,128)} fusion(bf16[4096,1280]{1,0:T(8,128)(2,1)} %param.6, f32[4096]{0:T(1024)S(1)} %add_rsqrt_fusion, bf16[1280,1920]{1,0:T(8,128)(2,1)} %reshape.662), kind=kOutput, calls=%fused_computation.9 | convolution fusion | flops 16792944640 | bytes 40976384 | tf_op jit(solution)/shard_map/dot_general | solution.py:108
  131.0 4.4 %slice.125 = bf16[4096,320]{0,1:T(8,128)(2,1)} slice(f32[4096,1600]{0,1:T(8,128)} %fusion.6), slice={[0:4096], [1280:1600]} | slice | bytes 5242880 | tf_op jit(solution)/shard_map/slice | solution.py:114
  135.4 10.4 %fusion.9 = bf16[4096,640]{0,1:T(8,128)(2,1)} fusion(f32[4096,1600]{0,1:T(8,128)} %fusion.6, f32[4096,80]{0,1:T(8,128)S(1)} %get-tuple-element.11, f32[4096,80]{0,1:T(8,128)S(1)} %get-tuple-element.10), kind=kLoop, calls=%fused_computation.12 | loop fusion | flops 10485760 | bytes 28835840 | tf_op jit(solution)/shard_map/convert_element_type | solution.py:111
  145.8 7.9 %copy.60 = bf16[4096,640]{1,0:T(8,128)(2,1)} copy(bf16[4096,640]{0,1:T(8,128)(2,1)} %fusion.9) | data formatting | bytes 10485760 | tf_op jit(solution)/shard_map/convert_element_type | solution.py:111
  153.7 3.5 copy.61
  157.2 5.4 %fusion.20 = f32[64,64,64]{1,2,0:T(8,128)S(1)} fusion(pred[320]{0:T(512)(128)(4,1)S(1)} %broadcast_compare_fusion.1, bf16[64,64,640]{2,1,0:T(8,128)(2,1)} %bitcast.54), kind=kOutput, calls=%fused_computation.28 | convolution fusion | flops 169082880 | bytes 7340352 | tf_op jit(solution)/shard_map/wqd,wkd->wqk/dot_general | solution.py:122
  170.1 5.4 %fusion.22 = f32[64,64,320]{2,1,0:T(8,128)} fusion(bf16[64,64,320]{2,1,0:T(8,128)(2,1)S(1)} %bitcast.50, pred[320]{0:T(512)(128)(4,1)S(1)} %broadcast_compare_fusion.3, f32[64,64]{1,0:T(8,128)S(1)} %fusion.127, f32[64,64,64]{1,2,0:T(8,128)} %copy-done.7), kind=kOutput, calls=%fused_computation.30 | convolution fusion | flops 170135616 | bytes 8929600 | tf_op jit(solution)/shard_map/wqk,wkd->wqd/dot_general | solution.py:129
  175.5 5.4 %fusion.14 = f32[64,64,320]{2,1,0:T(8,128)} fusion(bf16[64,64,320]{2,1,0:T(8,128)(2,1)S(1)} %bitcast.51, pred[320]{0:T(512)(128)(4,1)S(1)} %broadcast_compare_fusion, f32[64,64]{1,0:T(8,128)S(1)} %fusion.125, f32[64,64,64]{1,2,0:T(8,128)} %copy-done.6), kind=kOutput, calls=%fused_computation.22 | convolution fusion | flops 170135616 | bytes 8929600 | tf_op jit(solution)/shard_map/wqk,wkd->wqd/dot_general | solution.py:129
  180.9 5.3 %fusion.18 = f32[64,64,320]{2,1,0:T(8,128)} fusion(bf16[64,64,320]{2,1,0:T(8,128)(2,1)S(1)} %bitcast.52, pred[320]{0:T(512)(128)(4,1)S(1)} %broadcast_compare_fusion.1, f32[64,64]{1,0:T(8,128)S(1)} %fusion.126, f32[64,64,64]{1,2,0:T(8,128)} %copy-done.5), kind=kOutput, calls=%fused_computation.26 | convolution fusion | flops 170135616 | bytes 8929600 | tf_op jit(solution)/shard_map/wqk,wkd->wqd/dot_general | solution.py:129
  186.2 9.9 %add_convert_fusion = bf16[64,64,320]{2,1,0:T(8,128)(2,1)S(1)} fusion(f32[64,64,320]{2,1,0:T(8,128)} %fusion.14, f32[64,64,320]{2,1,0:T(8,128)} %fusion.18, f32[64,64,320]{2,1,0:T(8,128)} %fusion.22, bf16[64,64,320]{2,1,0:T(8,128)(2,1)} %bitcast.53, pred[320]{0:T(512)(128)(4,1)S(1)} %broadcast_compare_fusion.2, f32[64,64]{1,0:T(8,128)S(1)} %fusion.128, ...), kind=kOutput, calls=%fused_computation.15 | convolution fusion | flops 175378496 | bytes 22036800 | tf_op jit(solution)/shard_map/wqk,wkd->wqd/dot_general | solution.py:129
  198.1 3.9 %all-to-all-start = ((bf16[64,4,16,320]{3,2,0,1:T(8,128)(2,1)}), bf16[64,4,16,320]{3,2,0,1:T(8,128)(2,1)S(1)}, u32[]{:S(2)}, u32[]{:S(2)}) async-start(bf16[64,4,16,320]{3,2,0,1:T(8,128)(2,1)} %copy.66), calls=%async_computation | async-start | bytes 6291456 | tf_op jit(solution)/shard_map/all_to_all | solution.py:134
  201.9 3.4 constant_dynamic-slice_fusion
  205.4 33.7 %all-to-all-done = bf16[64,4,16,320]{3,2,0,1:T(8,128)(2,1)S(1)} async-done(((bf16[64,4,16,320]{3,2,0,1:T(8,128)(2,1)}), bf16[64,4,16,320]{3,2,0,1:T(8,128)(2,1)S(1)}, u32[]{:S(2)}, u32[]{:S(2)}) %all-to-all-start) | async-done | bytes 2621472 | tf_op jit(solution)/shard_map/all_to_all | solution.py:134
  239.0 7.3 %fusion.11 = bf16[1024,1280]{1,0:T(8,128)(2,1)} fusion(bf16[1024,1280]{1,0:T(8,128)(2,1)} %bitcast.59, bf16[1024,4,320]{2,0,1:T(8,128)(2,1)S(1)} %bitcast.58, bf16[1280,4,320]{0,2,1:T(8,128)(2,1)} %bitcast.63), kind=kOutput, calls=%fused_computation.18 | convolution fusion | flops 3359375360 | bytes 11141120 | tf_op jit(solution)/shard_map/dot_general | solution.py:136
  246.3 6.1 %reshape.648 = bf16[64,16,4,320]{3,2,1,0:T(4,128)(2,1)S(1)} reshape(bf16[1024,1280]{1,0:T(8,128)(2,1)} %fusion.11) | data formatting | bytes 5242880 | tf_op jit(solution)/shard_map/reshape | solution.py:145
  254.8 7.8 %all-to-all-start.1 = ((bf16[256,16,320]{2,1,0:T(8,128)(2,1)}), bf16[256,16,320]{2,1,0:T(8,128)(2,1)S(1)}, u32[]{:S(2)}, u32[]{:S(2)}) async-start(bf16[256,16,320]{2,1,0:T(8,128)(2,1)} %bitcast.48), calls=%async_computation.1 | async-start | bytes 6291456 | tf_op jit(solution)/shard_map/all_to_all | solution.py:149
  270.6 67.9 %all-to-all-done.1 = bf16[256,16,320]{2,1,0:T(8,128)(2,1)S(1)} async-done(((bf16[256,16,320]{2,1,0:T(8,128)(2,1)}), bf16[256,16,320]{2,1,0:T(8,128)(2,1)S(1)}, u32[]{:S(2)}, u32[]{:S(2)}) %all-to-all-start.1) | async-done | bytes 2621472 | tf_op jit(solution)/shard_map/all_to_all | solution.py:149
  338.6 2.7 gather_fusion
  341.3 5.0 %fusion.13 = bf16[4096,320]{1,0:T(8,128)(2,1)S(1)} fusion(bf16[256,16,320]{2,1,0:T(8,128)(2,1)} %gather_fusion, pred[4096]{0:T(1024)(128)(4,1)S(1)} %broadcast_in_dim.141, pred[4096]{0:T(1024)(128)(4,1)S(1)} %broadcast_in_dim.135), kind=kLoop, calls=%fused_computation.21 | loop fusion | flops 2621440 | bytes 5251072 | tf_op jit(solution)/shard_map/vmap(jit(_where))/select_n | solution.py:161
  346.3 2.7 copy.70
  (74 shorter events, 25.4 us)
Async XLA Ops:
  6.5 88.3 %all-gather.6.cloned.1.call-start = ((), (), s32[]{:S(2)}) async-start(), calls=%async_computation.3 | async-start | bytes 5990400 | tf_op jit(solution)/shard_map/all_gather | solution.py:96
  10.2 228.8 %all-gather.4.cloned.1.call-start = ((), (), s32[]{:S(2)}) async-start(), calls=%async_computation.2 | async-start | bytes 4096000 | tf_op jit(solution)/shard_map/all_gather | solution.py:99
  157.2 23.6 %copy-start = (bf16[4096,320]{1,0:T(8,128)(2,1)}, bf16[4096,320]{1,0:T(8,128)(2,1)S(1)}, u32[]{:S(2)}) copy-start(bf16[4096,320]{1,0:T(8,128)(2,1)S(1)} %copy.61) | copy-start | bytes 7864324
  157.2 6.7 %copy-start.1 = (bf16[4096,640]{1,0:T(8,128)(2,1)S(1)}, bf16[4096,640]{1,0:T(8,128)(2,1)}, u32[]{:S(2)}) copy-start(bf16[4096,640]{1,0:T(8,128)(2,1)} %copy.60) | copy-start | bytes 15728644
  162.6 1.4 copy-start.5
  165.3 2.8 copy-start.6
  166.7 2.7 copy-start.2
  168.1 2.0 copy-start.7
  198.1 41.0 %all-to-all-start = ((bf16[64,4,16,320]{3,2,0,1:T(8,128)(2,1)}), bf16[64,4,16,320]{3,2,0,1:T(8,128)(2,1)S(1)}, u32[]{:S(2)}, u32[]{:S(2)}) async-start(bf16[64,4,16,320]{3,2,0,1:T(8,128)(2,1)} %copy.66), calls=%async_computation | async-start | bytes 6291456 | tf_op jit(solution)/shard_map/all_to_all | solution.py:134
  254.8 7.8 %copy-start.3 = (s32[64]{0:T(128)S(1)}, s32[64]{0:T(128)}, u32[]{:S(2)}) copy-start(s32[64]{0:T(128)} %param.10) | copy-start | bytes 772
  254.8 11.0 %copy-start.4 = (s32[64]{0:T(128)S(1)}, s32[64]{0:T(128)}, u32[]{:S(2)}) copy-start(s32[64]{0:T(128)} %param.9) | copy-start | bytes 772
  254.8 83.8 %all-to-all-start.1 = ((bf16[256,16,320]{2,1,0:T(8,128)(2,1)}), bf16[256,16,320]{2,1,0:T(8,128)(2,1)S(1)}, u32[]{:S(2)}, u32[]{:S(2)}) async-start(bf16[256,16,320]{2,1,0:T(8,128)(2,1)} %bitcast.48), calls=%async_computation.1 | async-start | bytes 6291456 | tf_op jit(solution)/shard_map/all_to_all | solution.py:149
Sparse Core Ops, SparseCore 0:
  10.4 84.3 all-gather.5
  107.3 39.4 all-gather.3
where the time goes:
time: 357 us; the launch traced here: 356 us
  waiting for transfers between devices  173 us (48%)
  matrix products  66.5 us (19%)
  local copies, waits for them, and re-layouts  54 us (15%)
  other arithmetic  31.8 us (9%)
  between operations  18.9 us (5%)
  starting transfers between devices  11.7 us (3%)
    all_gather x1, waiting for transfers between devices, local(): joined = lax.all_gather(fused_rows, 'seq', axis=0, tiled=True)  71.3 us
    all_to_all x1, waiting for transfers between devices, local(): lax.all_to_all(sectioned, ('seq', 'mp'), split_axis=0, concat_axis=0, til...  67.9 us
    all_to_all x1, waiting for transfers between devices, local(): lax.all_to_all(spread, 'mp', split_axis=1, concat_axis=1, tiled=True)  33.7 us
    dot_general x4, matrix products, local(): jnp.einsum('wqk,wkd->wqd', weights, own_values, preferred_element_type=jn...  26 us
    dot_general x1, matrix products, local(): projected = jnp.dot(normed, fused, preferred_element_type=jnp.float32)  23.8 us
    convert_element_type x1, other arithmetic, local(): turned.astype(jnp.bfloat16).reshape(windows, window_tokens, 2 * width)  10.4 us
    dot_general x4, matrix products, local(): jnp.einsum('wqd,wkd->wqk', picked, key_block, preferred_element_type=jnp....  9.45 us
    reshape x2, local copies, waits for them, and re-layouts, local(): block_out.reshape(page_count, quarter_tokens, QUARTERS, share_width)  8.5 us
  transfers between devices with their start and end apart: 4, of which 3 were waited for; matrix products, arithmetic and copies ran while one was open for 31% of the time, Pallas kernels for 0%

commit v1 on v0

--- a/solution.py
+++ b/solution.py
@@ -93,7 +93,10 @@
         ],
         axis=1,
     )
-    joined = lax.all_gather(fused_rows, "seq", axis=0, tiled=True)
+    n_dev = lax.axis_size("seq")
+    parts = jnp.stack([fused_rows for _ in range(n_dev)])
+    parts = lax.all_to_all(parts, "seq", split_axis=0, concat_axis=0)
+    joined = jnp.concatenate(parts, axis=0)
     fused = joined[:, : 5 * heads * HD]
     out_rows_t = joined[:, 5 * heads * HD :]
     out_full_t = lax.all_gather(out_rows_t, "mp", axis=1, tiled=True)

time: 357 us -> 420 us (1.18)
  waiting for transfers between devices: 173 us -> 218 us
  starting transfers between devices: 11.7 us -> 29.3 us
    all_to_all x0 -> x1, waiting for transfers between devices: none -> 118 us  [local(): parts = lax.all_to_all(parts, 'seq', split_axis=0, concat_axis=0)]
    all_gather x1 -> x0, waiting for transfers between devices: 71.3 us -> none  [local(): joined = lax.all_gather(fused_rows, 'seq', axis=0, tiled=True)]
    all_to_all x0 -> x1, starting transfers between devices: none -> 13.4 us  [local(): parts = lax.all_to_all(parts, 'seq', split_axis=0, concat_axis=0)]
    reshape x0 -> x1, local copies, waits for them, and re-layouts: none -> 7.54 us  [local(): joined = jnp.concatenate(parts, axis=0)]
    unnamed x18 -> x19, local copies, waits for them, and re-layouts: 8.29 us -> 0.76 us
  transfers between devices with their start and end apart: 4 -> 4, of which waited for: 3 -> 3; matrix products, arithmetic and copies ran while one was open for 31% -> 26% of each run, Pallas kernels for 0% -> 0%
where the time goes in v1:
time: 420 us; the launch traced here: 419 us
  waiting for transfers between devices  218 us (52%)
  matrix products  66.6 us (16%)
  local copies, waits for them, and re-layouts  55.7 us (13%)
  other arithmetic  30.5 us (7%)
  starting transfers between devices  29.3 us (7%)
  between operations  18.9 us (4%)
    all_to_all x1, waiting for transfers between devices, local(): parts = lax.all_to_all(parts, 'seq', split_axis=0, concat_axis=0)  118 us
    all_to_all x1, waiting for transfers between devices, local(): lax.all_to_all(sectioned, ('seq', 'mp'), split_axis=0, concat_axis=0, til...  68.6 us
    all_to_all x1, waiting for transfers between devices, local(): lax.all_to_all(spread, 'mp', split_axis=1, concat_axis=1, tiled=True)  31.1 us
    dot_general x4, matrix products, local(): jnp.einsum('wqk,wkd->wqd', weights, own_values, preferred_element_type=jn...  26 us
    dot_general x1, matrix products, local(): projected = jnp.dot(normed, fused, preferred_element_type=jnp.float32)  23.8 us
    all_to_all x1, starting transfers between devices, local(): parts = lax.all_to_all(parts, 'seq', split_axis=0, concat_axis=0)  13.4 us
    all_to_all x1, starting transfers between devices, local(): lax.all_to_all(sectioned, ('seq', 'mp'), split_axis=0, concat_axis=0, til...  11.7 us
    convert_element_type x1, other arithmetic, local(): turned.astype(jnp.bfloat16).reshape(windows, window_tokens, 2 * width)  10.4 us
  transfers between devices with their start and end apart: 4, of which 3 were waited for; matrix products, arithmetic and copies ran while one was open for 26% of the time, Pallas kernels for 0%

profile of v1, /device:TPU:1, one launch (start us, length us, event | category | flops | bytes accessed | tf_op | source)
XLA Modules:
  0.0 419.1 jit_solution(13290080205929699210)
XLA Ops:
  9.6 3.0 stack.2
  12.6 13.4 %all-to-all-start = ((bf16[64,20,1920]{2,1,0:T(8,128)(2,1)}), bf16[64,20,1920]{2,1,0:T(8,128)(2,1)}, u32[]{:S(2)}, u32[]{:S(2)}) async-start(bf16[64,20,1920]{2,1,0:T(8,128)(2,1)} %stack.2), calls=%async_computation | async-start | bytes 11796480 | tf_op jit(solution)/shard_map/all_to_all | solution.py:98
  27.0 6.1 %fusion.4 = f32[4096]{0:T(1024)S(1)} fusion(bf16[4096,1280]{1,0:T(8,128)(2,1)} %param.6), kind=kLoop, calls=%fused_computation.7 | loop fusion | flops 15724544 | bytes 10502144 | tf_op jit(solution)/shard_map/reduce_sum | solution.py:60
  33.3 4.8 %fusion.69 = (f32[4096,80]{0,1:T(8,128)S(1)}, f32[4096,80]{0,1:T(8,128)S(1)}) fusion(f32[4096,20]{0,1:T(8,128)S(1)} %get-tuple-element.19, f32[4096,20]{0,1:T(8,128)S(1)} %get-tuple-element.18), kind=kLoop, calls=%fused_computation.88 | loop fusion | flops 983040 | bytes 3276800 | tf_op jit(solution)/shard_map/cos | solution.py:23
  38.0 118.5 %all-to-all-done = bf16[64,20,1920]{2,1,0:T(8,128)(2,1)} async-done(((bf16[64,20,1920]{2,1,0:T(8,128)(2,1)}), bf16[64,20,1920]{2,1,0:T(8,128)(2,1)}, u32[]{:S(2)}, u32[]{:S(2)}) %all-to-all-start) | async-done | bytes 4915232 | tf_op jit(solution)/shard_map/all_to_all | solution.py:98
  156.5 7.5 %reshape.649 = bf16[1280,1920]{1,0:T(8,128)(2,1)} reshape(bf16[64,20,1920]{2,1,0:T(8,128)(2,1)} %all-to-all-done) | data formatting | bytes 9830400 | tf_op jit(solution)/shard_map/reshape | solution.py:99
  168.9 23.8 %fusion.6 = f32[4096,1600]{0,1:T(8,128)} fusion(bf16[4096,1280]{1,0:T(8,128)(2,1)} %param.6, f32[4096]{0:T(1024)S(1)} %add_rsqrt_fusion, bf16[1280,1920]{1,0:T(8,128)(2,1)} %reshape.649), kind=kOutput, calls=%fused_computation.9 | convolution fusion | flops 16792944640 | bytes 40976384 | tf_op jit(solution)/shard_map/dot_general | solution.py:111
  192.8 4.4 %slice.125 = bf16[4096,320]{0,1:T(8,128)(2,1)} slice(f32[4096,1600]{0,1:T(8,128)} %fusion.6), slice={[0:4096], [1280:1600]} | slice | bytes 5242880 | tf_op jit(solution)/shard_map/slice | solution.py:117
  197.2 10.4 %fusion.9 = bf16[4096,640]{0,1:T(8,128)(2,1)} fusion(f32[4096,1600]{0,1:T(8,128)} %fusion.6, f32[4096,80]{0,1:T(8,128)S(1)} %get-tuple-element.11, f32[4096,80]{0,1:T(8,128)S(1)} %get-tuple-element.10), kind=kLoop, calls=%fused_computation.12 | loop fusion | flops 10485760 | bytes 28835840 | tf_op jit(solution)/shard_map/convert_element_type | solution.py:114
  207.6 7.9 %copy.60 = bf16[4096,640]{1,0:T(8,128)(2,1)} copy(bf16[4096,640]{0,1:T(8,128)(2,1)} %fusion.9) | data formatting | bytes 10485760 | tf_op jit(solution)/shard_map/convert_element_type | solution.py:114
  215.5 3.5 copy.61
  219.1 5.4 %fusion.20 = f32[64,64,64]{1,2,0:T(8,128)S(1)} fusion(pred[320]{0:T(512)(128)(4,1)S(1)} %broadcast_compare_fusion.1, bf16[64,64,640]{2,1,0:T(8,128)(2,1)} %bitcast.53), kind=kOutput, calls=%fused_computation.28 | convolution fusion | flops 169082880 | bytes 7340352 | tf_op jit(solution)/shard_map/wqd,wkd->wqk/dot_general | solution.py:125
  231.9 5.4 %fusion.22 = f32[64,64,320]{2,1,0:T(8,128)} fusion(bf16[64,64,320]{2,1,0:T(8,128)(2,1)S(1)} %bitcast.49, pred[320]{0:T(512)(128)(4,1)S(1)} %broadcast_compare_fusion.3, f32[64,64]{1,0:T(8,128)S(1)} %fusion.127, f32[64,64,64]{1,2,0:T(8,128)} %copy-done.8), kind=kOutput, calls=%fused_computation.30 | convolution fusion | flops 170135616 | bytes 8929600 | tf_op jit(solution)/shard_map/wqk,wkd->wqd/dot_general | solution.py:132
  237.3 5.4 %fusion.14 = f32[64,64,320]{2,1,0:T(8,128)} fusion(bf16[64,64,320]{2,1,0:T(8,128)(2,1)S(1)} %bitcast.50, pred[320]{0:T(512)(128)(4,1)S(1)} %broadcast_compare_fusion, f32[64,64]{1,0:T(8,128)S(1)} %fusion.125, f32[64,64,64]{1,2,0:T(8,128)} %copy-done.7), kind=kOutput, calls=%fused_computation.22 | convolution fusion | flops 170135616 | bytes 8929600 | tf_op jit(solution)/shard_map/wqk,wkd->wqd/dot_general | solution.py:132
  242.7 5.3 %fusion.18 = f32[64,64,320]{2,1,0:T(8,128)} fusion(bf16[64,64,320]{2,1,0:T(8,128)(2,1)S(1)} %bitcast.51, pred[320]{0:T(512)(128)(4,1)S(1)} %broadcast_compare_fusion.1, f32[64,64]{1,0:T(8,128)S(1)} %fusion.126, f32[64,64,64]{1,2,0:T(8,128)} %copy-done.6), kind=kOutput, calls=%fused_computation.26 | convolution fusion | flops 170135616 | bytes 8929600 | tf_op jit(solution)/shard_map/wqk,wkd->wqd/dot_general | solution.py:132
  248.0 9.9 %add_convert_fusion = bf16[64,64,320]{2,1,0:T(8,128)(2,1)S(1)} fusion(f32[64,64,320]{2,1,0:T(8,128)} %fusion.14, f32[64,64,320]{2,1,0:T(8,128)} %fusion.18, f32[64,64,320]{2,1,0:T(8,128)} %fusion.22, bf16[64,64,320]{2,1,0:T(8,128)(2,1)} %bitcast.52, pred[320]{0:T(512)(128)(4,1)S(1)} %broadcast_compare_fusion.2, f32[64,64]{1,0:T(8,128)S(1)} %fusion.128, ...), kind=kOutput, calls=%fused_computation.15 | convolution fusion | flops 175378496 | bytes 22036800 | tf_op jit(solution)/shard_map/wqk,wkd->wqd/dot_general | solution.py:132
  259.9 3.9 all-to-all-start.1
  263.9 3.4 constant_dynamic-slice_fusion
  267.3 31.1 %all-to-all-done.1 = bf16[64,4,16,320]{3,2,0,1:T(8,128)(2,1)S(1)} async-done(((bf16[64,4,16,320]{3,2,0,1:T(8,128)(2,1)}), bf16[64,4,16,320]{3,2,0,1:T(8,128)(2,1)S(1)}, u32[]{:S(2)}, u32[]{:S(2)}) %all-to-all-start.1) | async-done | bytes 2621472 | tf_op jit(solution)/shard_map/all_to_all | solution.py:137
  298.4 7.3 %fusion.11 = bf16[1024,1280]{1,0:T(8,128)(2,1)} fusion(bf16[1024,1280]{1,0:T(8,128)(2,1)} %bitcast.58, bf16[1024,4,320]{2,0,1:T(8,128)(2,1)S(1)} %bitcast.57, bf16[1280,4,320]{0,2,1:T(8,128)(2,1)} %bitcast.61), kind=kOutput, calls=%fused_computation.18 | convolution fusion | flops 3359375360 | bytes 11141120 | tf_op jit(solution)/shard_map/dot_general | solution.py:139
  305.7 6.1 %reshape.654 = bf16[64,16,4,320]{3,2,1,0:T(4,128)(2,1)S(1)} reshape(bf16[1024,1280]{1,0:T(8,128)(2,1)} %fusion.11) | data formatting | bytes 5242880 | tf_op jit(solution)/shard_map/reshape | solution.py:148
  314.2 11.7 %all-to-all-start.2 = ((bf16[256,16,320]{2,1,0:T(8,128)(2,1)}), bf16[256,16,320]{2,1,0:T(8,128)(2,1)S(1)}, u32[]{:S(2)}, u32[]{:S(2)}) async-start(bf16[256,16,320]{2,1,0:T(8,128)(2,1)} %bitcast.47), calls=%async_computation.2 | async-start | bytes 6291456 | tf_op jit(solution)/shard_map/all_to_all | solution.py:152
  333.2 68.6 %all-to-all-done.2 = bf16[256,16,320]{2,1,0:T(8,128)(2,1)S(1)} async-done(((bf16[256,16,320]{2,1,0:T(8,128)(2,1)}), bf16[256,16,320]{2,1,0:T(8,128)(2,1)S(1)}, u32[]{:S(2)}, u32[]{:S(2)}) %all-to-all-start.2) | async-done | bytes 2621472 | tf_op jit(solution)/shard_map/all_to_all | solution.py:152
  404.5 5.0 %fusion.13 = bf16[4096,320]{1,0:T(8,128)(2,1)S(1)} fusion(bf16[256,16,320]{2,1,0:T(8,128)(2,1)} %gather_fusion, pred[4096]{0:T(1024)(128)(4,1)S(1)} %broadcast_in_dim.141, pred[4096]{0:T(1024)(128)(4,1)S(1)} %broadcast_in_dim.135), kind=kLoop, calls=%fused_computation.21 | loop fusion | flops 2621440 | bytes 5251072 | tf_op jit(solution)/shard_map/vmap(jit(_where))/select_n | solution.py:164
  (76 shorter events, 28.3 us)
Async XLA Ops:
  12.6 13.7 %copy-start.3 = (s32[64,64]{1,0:T(8,128)S(1)}, s32[64,64]{1,0:T(8,128)}, u32[]{:S(2)}) copy-start(s32[64,64]{1,0:T(8,128)} %param.11) | copy-start | bytes 49156
  12.6 13.8 %copy-start.4 = (s32[64]{0:T(128)S(1)}, s32[64]{0:T(128)}, u32[]{:S(2)}) copy-start(s32[64]{0:T(128)} %param.10) | copy-start | bytes 772
  12.6 144.0 %all-to-all-start = ((bf16[64,20,1920]{2,1,0:T(8,128)(2,1)}), bf16[64,20,1920]{2,1,0:T(8,128)(2,1)}, u32[]{:S(2)}, u32[]{:S(2)}) async-start(bf16[64,20,1920]{2,1,0:T(8,128)(2,1)} %stack.2), calls=%async_computation | async-start | bytes 11796480 | tf_op jit(solution)/shard_map/all_to_all | solution.py:98
  26.0 272.4 %all-gather.2.cloned.1.call-start = ((), (), s32[]{:S(2)}) async-start(), calls=%async_computation.3 | async-start | bytes 4096000 | tf_op jit(solution)/shard_map/all_gather | solution.py:102
  219.1 23.6 %copy-start = (bf16[4096,320]{1,0:T(8,128)(2,1)}, bf16[4096,320]{1,0:T(8,128)(2,1)S(1)}, u32[]{:S(2)}) copy-start(bf16[4096,320]{1,0:T(8,128)(2,1)S(1)} %copy.61) | copy-start | bytes 7864324
  219.1 6.7 %copy-start.1 = (bf16[4096,640]{1,0:T(8,128)(2,1)S(1)}, bf16[4096,640]{1,0:T(8,128)(2,1)}, u32[]{:S(2)}) copy-start(bf16[4096,640]{1,0:T(8,128)(2,1)} %copy.60) | copy-start | bytes 15728644
  224.4 1.4 copy-start.6
  227.2 2.8 copy-start.7
  228.6 2.7 copy-start.2
  230.0 2.0 copy-start.8
  259.9 38.5 %all-to-all-start.1 = ((bf16[64,4,16,320]{3,2,0,1:T(8,128)(2,1)}), bf16[64,4,16,320]{3,2,0,1:T(8,128)(2,1)S(1)}, u32[]{:S(2)}, u32[]{:S(2)}) async-start(bf16[64,4,16,320]{3,2,0,1:T(8,128)(2,1)} %copy.66), calls=%async_computation.1 | async-start | bytes 6291456 | tf_op jit(solution)/shard_map/all_to_all | solution.py:137
  314.2 14.9 %copy-start.5 = (s32[64]{0:T(128)S(1)}, s32[64]{0:T(128)}, u32[]{:S(2)}) copy-start(s32[64]{0:T(128)} %param.9) | copy-start | bytes 772
  314.2 87.6 %all-to-all-start.2 = ((bf16[256,16,320]{2,1,0:T(8,128)(2,1)}), bf16[256,16,320]{2,1,0:T(8,128)(2,1)S(1)}, u32[]{:S(2)}, u32[]{:S(2)}) async-start(bf16[256,16,320]{2,1,0:T(8,128)(2,1)} %bitcast.47), calls=%async_computation.2 | async-start | bytes 6291456 | tf_op jit(solution)/shard_map/all_to_all | solution.py:152
Sparse Core Ops, SparseCore 0:
  169.0 41.2 all-gather.1
